TPU v7x, 512 devices: a whole 4x4x16 slice. The times are simulated.
512 devices in a mesh: aux: 16 (over z), pair: 32 (over y, x, core).
Axes of the slice: x: 4, y: 4, z: 16, core: 2. Of those that a mesh axis runs over, the one named last changes fastest.
Arguments:
- b_tensor: bfloat16 [2560, 262144], P('aux', 'pair'), may hold values from -0.0625 to 0.0625
- eps_occ: float32 [256], replicated, may hold values from -1 to -0.3
- eps_vir: float32 [1024], replicated, may hold values from 0.05 to 3
- trial: bfloat16 [32, 262144], P(None, 'pair'), may hold values from -6 to 6
Outputs:
- trial_next: float32 [32, 262144], P(None, 'pair')
- residual: bfloat16 [32, 262144], P(None, 'pair')
- subspace: float32 [32, 32], replicated
All inputs are finite; a program needn't handle non-finite values.
Results may differ from a plain program's by a relative error of at most 0.028.
Values may be sent and summed in bfloat16 or wider, within the bound.
No kernel may reach another device: no remote copies, remote signals or barrier semaphores. Data moves between devices by JAX's collectives and lax.ppermute only.
A program may use at most 64 MiB of HBM per device.

v0:
```python
import jax
import jax.numpy as jnp
from jax import lax
from jax.sharding import PartitionSpec as P

ITERS = 2
HIGHEST_PRECISION = lax.Precision.HIGHEST


def correlation_of(first_rows, second_rows, precision=HIGHEST_PRECISION):
    return lax.dot_general(
        first_rows,
        second_rows,
        (((1,), (1,)), ((), ())),
        precision=precision,
        preferred_element_type=jnp.float32,
    )


def product(first_mat, second_mat):
    return jnp.dot(
        first_mat, second_mat, precision=HIGHEST_PRECISION, preferred_element_type=jnp.float32
    )


def pair_sum(matrices):
    return lax.all_gather(matrices, "pair").sum(0)


def aux_sum(terms):
    n_aux = lax.axis_size("aux")
    rows, cols = terms.shape
    pieces = terms.reshape(rows, n_aux, cols // n_aux)
    pieces = lax.all_to_all(pieces, "aux", 1, 1, tiled=True)
    mine = pieces.astype(jnp.float32).sum(1)
    return lax.all_gather(mine, "aux", axis=1, tiled=True)


def inverse_factor(gram_now):
    lower_tri = jnp.linalg.cholesky(gram_now)
    return lax.linalg.triangular_solve(
        lower_tri, jnp.eye(gram_now.shape[0], dtype=jnp.float32), left_side=True, lower=True
    )


def on_device(b_tensor, eps_occ, eps_vir, trial):
    block_cols = b_tensor.shape[1]
    npair_all = eps_occ.shape[0] * eps_vir.shape[0]
    k = trial.shape[0]
    everything = (eps_vir[None, :] - eps_occ[:, None]).reshape(npair_all)
    diagonal = lax.dynamic_slice_in_dim(everything, lax.axis_index("pair") * block_cols, block_cols)
    diag_row = diagonal[None, :]
    trial_now = trial
    for iteration in range(ITERS):
        if iteration == 0:
            gram_part = correlation_of(trial_now, trial_now, None)
            cross_part = correlation_of(b_tensor, trial_now, None)
        else:
            gram_part = correlation_of(trial_now, trial_now)
            cross_part = correlation_of(b_tensor.astype(jnp.float32), trial_now)
        summed = pair_sum(jnp.concatenate([gram_part / npair_all, cross_part], axis=0))
        inverse = inverse_factor(summed[:k])
        basis_now = product(inverse, trial_now.astype(jnp.float32))
        projected = lax.dot_general(
            summed[k:],
            inverse,
            (((1,), (1,)), ((), ())),
            precision=HIGHEST_PRECISION,
            preferred_element_type=jnp.float32,
        )
        projected_low = projected.astype(jnp.bfloat16)
        term = lax.dot_general(
            projected_low, b_tensor, (((0,), (0,)), ((), ())), preferred_element_type=jnp.float32
        ).astype(jnp.bfloat16)
        image_now = aux_sum(term) + diag_row * basis_now
        subspace = pair_sum(correlation_of(image_now, basis_now) / npair_all)
        residual = image_now - product(subspace, basis_now)
        trial_now = basis_now - residual / diag_row
    return (trial_now, residual.astype(jnp.bfloat16), subspace)


def solution(mesh):
    in_specs = (P("aux", "pair"), P(), P(), P(None, "pair"))
    out_specs = (P(None, "pair"), P(None, "pair"), P())
    return jax.shard_map(
        on_device, mesh=mesh, in_specs=in_specs, out_specs=out_specs, check_vma=False
    )
```

profile of v0, /device:TPU:1, one launch (start us, length us, event | category | flops | bytes accessed | tf_op | source)
XLA Modules:
  0.0 371.0 jit_solution(16617916019839826232)
XLA Ops:
  7.2 1.6 convolution_multiply_fusion.3
  9.2 2.0 fusion.19
  11.3 31.4 %all-gather.4 = f32[32,192,32]{1,2,0:T(8,128)} all-gather(f32[1,192,32]{1,2,0:T(8,128)S(1)} %maximum_bitcast_fusion), channel_id=2, replica_groups=mesh['aux'=16,'pair'=32] {'pair'}, dimensions={0}, use_global_device_ids=true | all-gather | bytes 811008 | tf_op jit(solution)/shard_map/all_gather | solution.py:27
  42.7 1.3 reduce_sum.54
  44.1 2.9 cholesky.44
  48.4 2.4 custom-call.6
  52.2 35.2 %all_to_all.10 = bf16[32,16,512]{2,0,1:T(8,128)(2,1)S(1)} all-to-all(bf16[32,16,512]{2,0,1:T(8,128)(2,1)S(1)} %bitcast.64), channel_id=1, replica_groups=mesh['aux'=16,'pair'=32] {'aux'}, dimensions={1} | all-to-all | bytes 1048576 | tf_op jit(solution)/shard_map/all_to_all | solution.py:34
  88.3 1.2 copy.28
  90.3 1.5 fusion.20
  91.8 57.8 %all-gather.9.cloned.1.call-done = f32[32,8192]{1,0:T(8,128)} async-done(((f32[32,512]{1,0:T(8,128)}), f32[32,8192]{1,0:T(8,128)}) %all-gather.9.cloned.1.call-update) | async-done | bytes 1048592 | tf_op jit(solution)/shard_map/all_gather | solution.py:36
  149.6 2.9 convolution_multiply_fusion.2
  152.6 34.8 %all-gather.1 = f32[1024,32]{1,0:T(8,128)S(1)} all-gather(f32[32,32]{1,0:T(8,128)S(1)} %copy.14), channel_id=3, replica_groups=mesh['aux'=16,'pair'=32] {'pair'}, dimensions={0}, use_global_device_ids=true | all-gather | bytes 135168 | tf_op jit(solution)/shard_map/all_gather | solution.py:27
  187.4 3.0 fusion.1
  190.5 2.4 convolution_bitcast_fusion
  194.0 26.7 %all-gather.5 = f32[32,192,32]{1,2,0:T(8,128)} all-gather(f32[1,192,32]{1,2,0:T(8,128)S(1)} %maximum_bitcast_fusion.1), channel_id=4, replica_groups=mesh['aux'=16,'pair'=32] {'pair'}, dimensions={0}, use_global_device_ids=true | all-gather | bytes 811008 | tf_op jit(solution)/shard_map/all_gather | solution.py:27
  220.7 1.3 reduce_sum.57
  222.1 2.9 cholesky.55
  226.3 2.4 custom-call.7
  230.1 30.5 %all_to_all.11 = bf16[32,16,512]{2,0,1:T(8,128)(2,1)S(1)} all-to-all(bf16[32,16,512]{2,0,1:T(8,128)(2,1)S(1)} %bitcast.66), channel_id=1, replica_groups=mesh['aux'=16,'pair'=32] {'aux'}, dimensions={1} | all-to-all | bytes 1048576 | tf_op jit(solution)/shard_map/all_to_all | solution.py:34
  261.3 3.2 fusion.21
  264.5 57.6 %all-gather.11.cloned.1.call-done = f32[32,8192]{1,0:T(8,128)} async-done(((f32[32,512]{1,0:T(8,128)}), f32[32,8192]{1,0:T(8,128)}) %all-gather.11.cloned.1.call-update) | async-done | bytes 1048592 | tf_op jit(solution)/shard_map/all_gather | solution.py:36
  322.1 2.9 convolution_multiply_fusion
  325.1 34.8 %all-gather.3 = f32[1024,32]{1,0:T(8,128)S(1)} all-gather(f32[32,32]{1,0:T(8,128)S(1)} %copy.19), channel_id=5, replica_groups=mesh['aux'=16,'pair'=32] {'pair'}, dimensions={0}, use_global_device_ids=true | all-gather | bytes 135168 | tf_op jit(solution)/shard_map/all_gather | solution.py:27
  360.0 4.2 %fusion.18 = (bf16[32,8192]{1,0:T(8,128)(2,1)}, f32[32,8192]{1,0:T(8,128)}) fusion(f32[32,8192]{1,0:T(8,128)} %fusion.21, f32[8192]{0:T(1024)S(1)} %dynamic_slice.3, f32[32,32]{1,0:T(8,128)S(1)} %reduce_sum.59, f32[32,8192]{1,0:T(8,128)} %all-gather.11.cloned.1.call-done), kind=kOutput, calls=%fused_computation.48 | convolution fusion | flops 102236160 | bytes 3706880 | tf_op jit(solution)/shard_map/dot_general | solution.py:21
  (47 shorter events, 9.6 us)
Async XLA Ops:
  7.2 2.1 copy-start
  7.2 142.5 %all-gather.9.cloned.1.call-start = ((), (), s32[]{:S(2)}) async-start(), calls=%async_computation.2 | async-start | bytes 1114112 | tf_op jit(solution)/shard_map/all_gather | solution.py:36
  51.4 36.7 %copy-start.4 = (f32[1024]{0:T(1024)S(1)}, f32[1024]{0:T(1024)}, u32[]{:S(2)}) copy-start(f32[1024]{0:T(1024)} %param.9) | copy-start | bytes 12292
  51.4 36.7 %copy-start.5 = (f32[256]{0:T(256)S(1)}, f32[256]{0:T(256)}, u32[]{:S(2)}) copy-start(f32[256]{0:T(256)} %param.8) | copy-start | bytes 3076
  52.2 38.1 %copy-start.2 = (bf16[32,8192]{1,0:T(8,128)(2,1)S(1)}, bf16[32,8192]{1,0:T(8,128)(2,1)}, u32[]{:S(2)}) copy-start(bf16[32,8192]{1,0:T(8,128)(2,1)} %param.10) | copy-start | bytes 1572868
  88.1 234.0 %all-gather.11.cloned.1.call-start = ((), (), s32[]{:S(2)}) async-start(), calls=%async_computation.3 | async-start | bytes 1114112 | tf_op jit(solution)/shard_map/all_gather | solution.py:36
  190.5 3.4 copy-start.1
  359.9 4.2 %copy-start.3 = (f32[32,32]{1,0:T(8,128)}, f32[32,32]{1,0:T(8,128)S(1)}, u32[]{:S(2)}) copy-start(f32[32,32]{1,0:T(8,128)S(1)} %reduce_sum.59) | copy-start | bytes 12292
Sparse Core Ops, SparseCore 0:
  88.2 61.3 all-gather.8
  261.4 60.6 all-gather.10
where the time goes:
time: 372 us; the launch traced here: 371 us
  blocking collectives  193 us (52%)
  waiting for transfers between devices  115 us (31%)
  matrix products  27.3 us (7%)
  other arithmetic  17.8 us (5%)
  between operations  14.3 us (4%)
    all_gather x4, blocking collectives, pair_sum(): return lax.all_gather(matrices, 'pair').sum(0)  128 us
    all_gather x2, waiting for transfers between devices, aux_sum(): return lax.all_gather(mine, 'aux', axis=1, tiled=True)  115 us
    all_to_all x2, blocking collectives, aux_sum(): pieces = lax.all_to_all(pieces, 'aux', 1, 1, tiled=True)  65.7 us
    dot_general x6, matrix products, correlation_of(): lax.dot_general(first_rows, second_rows, (((1,), (1,)), ((), ())), precis...  12.8 us
    dot_general x4, matrix products, product(): jnp.dot(first_mat, second_mat, precision=HIGHEST_PRECISION, preferred_ele...  12 us
  transfers between devices with their start and end apart: 2, of which 2 were waited for; matrix products, arithmetic and copies ran while one was open for 2% of the time, Pallas kernels for 0%

commit v1 on v0

--- a/solution.py
+++ b/solution.py
@@ -5,6 +5,16 @@
 
 ITERS = 2
 HIGHEST_PRECISION = lax.Precision.HIGHEST
+
+
+def number_the_face(z_in, shard_axis):
+    carry_out = jnp.concatenate(
+        lax.all_to_all(
+            jnp.stack([z_in for _ in range(lax.axis_size(shard_axis))], 0), shard_axis, 0, 0
+        ),
+        1,
+    )
+    return carry_out
 
 
 def correlation_of(first_rows, second_rows, precision=HIGHEST_PRECISION):
@@ -33,7 +43,7 @@
     pieces = terms.reshape(rows, n_aux, cols // n_aux)
     pieces = lax.all_to_all(pieces, "aux", 1, 1, tiled=True)
     mine = pieces.astype(jnp.float32).sum(1)
-    return lax.all_gather(mine, "aux", axis=1, tiled=True)
+    return number_the_face(mine, "aux")
 
 
 def inverse_factor(gram_now):

time: 372 us -> 342 us (0.919)
  waiting for transfers between devices: 115 us -> 83.8 us
  starting transfers between devices: 0.08 us -> 25.4 us
  between operations: 14.3 us -> 0.91 us
  blocking collectives: 193 us -> 181 us
  local copies, waits for them, and re-layouts: 2.75 us -> 9.82 us
    all_gather x2 -> x0, waiting for transfers between devices: 115 us -> none  [aux_sum(): return lax.all_gather(mine, 'aux', axis=1, tiled=True)]
    all_to_all x0 -> x2, waiting for transfers between devices: none -> 83.8 us  [number_the_face(): lax.all_to_all(jnp.stack([z_in for _ in range(lax.axis_size(shard_axis))]...]
    all_to_all x0 -> x2, starting transfers between devices: none -> 25.4 us  [number_the_face(): lax.all_to_all(jnp.stack([z_in for _ in range(lax.axis_size(shard_axis))]...]
    all_gather x4, blocking collectives: 128 us -> 116 us  [pair_sum(): return lax.all_gather(matrices, 'pair').sum(0)]
where the time goes in v1:
time: 342 us; the launch traced here: 341 us
  blocking collectives  181 us (53%)
  waiting for transfers between devices  83.8 us (25%)
  starting transfers between devices  25.4 us (7%)
  matrix products  23.7 us (7%)
  other arithmetic  16.5 us (5%)
  local copies, waits for them, and re-layouts  9.82 us (3%)
    all_gather x4, blocking collectives, pair_sum(): return lax.all_gather(matrices, 'pair').sum(0)  116 us
    all_to_all x2, waiting for transfers between devices, number_the_face(): lax.all_to_all(jnp.stack([z_in for _ in range(lax.axis_size(shard_axis))]...  83.8 us
    all_to_all x2, blocking collectives, aux_sum(): pieces = lax.all_to_all(pieces, 'aux', 1, 1, tiled=True)  65.6 us
    all_to_all x2, starting transfers between devices, number_the_face(): lax.all_to_all(jnp.stack([z_in for _ in range(lax.axis_size(shard_axis))]...  25.4 us
    dot_general x4, matrix products, product(): jnp.dot(first_mat, second_mat, precision=HIGHEST_PRECISION, preferred_ele...  12.1 us
    dot_general x6, matrix products, correlation_of(): lax.dot_general(first_rows, second_rows, (((1,), (1,)), ((), ())), precis...  9.09 us
    another operation x6, other arithmetic, inverse_factor(): lower_tri = jnp.linalg.cholesky(gram_now)  7.19 us
  transfers between devices with their start and end apart: 2, of which 2 were waited for; matrix products, arithmetic and copies ran while one was open for 2% of the time, Pallas kernels for 0%

profile of v1, /device:TPU:1, one launch (start us, length us, event | category | flops | bytes accessed | tf_op | source)
XLA Modules:
  0.0 341.3 jit_solution(15371869226992699163)
XLA Ops:
  0.6 1.6 convolution_multiply_fusion.3
  2.7 2.0 fusion.19
  4.7 31.4 %all-gather.4 = f32[32,192,32]{1,2,0:T(8,128)} all-gather(f32[1,192,32]{1,2,0:T(8,128)S(1)} %maximum_bitcast_fusion), channel_id=2, replica_groups=mesh['aux'=16,'pair'=32] {'pair'}, dimensions={0}, use_global_device_ids=true | all-gather | bytes 811008 | tf_op jit(solution)/shard_map/all_gather | solution.py:37
  37.6 2.9 cholesky.44
  41.8 2.4 custom-call.6
  45.6 35.1 %all_to_all.20 = bf16[32,16,512]{2,0,1:T(8,128)(2,1)S(1)} all-to-all(bf16[32,16,512]{2,0,1:T(8,128)(2,1)S(1)} %bitcast.74), channel_id=1, replica_groups=mesh['aux'=16,'pair'=32] {'aux'}, dimensions={1} | all-to-all | bytes 1048576 | tf_op jit(solution)/shard_map/all_to_all | solution.py:44
  82.0 12.7 %all-to-all-start.1 = ((f32[16,32,512]{2,1,0:T(8,128)}), f32[16,32,512]{2,1,0:T(8,128)}, u32[]{:S(2)}, u32[]{:S(2)}) async-start(f32[16,32,512]{2,1,0:T(8,128)} %stack.4), calls=%async_computation.1 | async-start | bytes 2097152 | tf_op jit(solution)/shard_map/all_to_all | solution.py:12
  96.8 1.5 fusion.20
  98.3 41.7 %all-to-all-done.1 = f32[16,32,512]{2,1,0:T(8,128)} async-done(((f32[16,32,512]{2,1,0:T(8,128)}), f32[16,32,512]{2,1,0:T(8,128)}, u32[]{:S(2)}, u32[]{:S(2)}) %all-to-all-start.1) | async-done | bytes 1048608 | tf_op jit(solution)/shard_map/all_to_all | solution.py:12
  140.0 1.4 copy.30
  143.6 29.6 %all-gather.1 = f32[1024,32]{1,0:T(8,128)S(1)} all-gather(f32[32,32]{1,0:T(8,128)S(1)} %copy.15), channel_id=3, replica_groups=mesh['aux'=16,'pair'=32] {'pair'}, dimensions={0}, use_global_device_ids=true | all-gather | bytes 135168 | tf_op jit(solution)/shard_map/all_gather | solution.py:37
  173.2 3.0 fusion.1
  176.2 2.4 convolution_bitcast_fusion
  179.7 25.1 %all-gather.5 = f32[32,192,32]{1,2,0:T(8,128)} all-gather(f32[1,192,32]{1,2,0:T(8,128)S(1)} %maximum_bitcast_fusion.1), channel_id=4, replica_groups=mesh['aux'=16,'pair'=32] {'pair'}, dimensions={0}, use_global_device_ids=true | all-gather | bytes 811008 | tf_op jit(solution)/shard_map/all_gather | solution.py:37
  204.8 1.3 reduce_sum.57
  206.2 2.9 cholesky.55
  210.5 2.4 custom-call.7
  214.3 30.5 %all_to_all.21 = bf16[32,16,512]{2,0,1:T(8,128)(2,1)S(1)} all-to-all(bf16[32,16,512]{2,0,1:T(8,128)(2,1)S(1)} %bitcast.76), channel_id=1, replica_groups=mesh['aux'=16,'pair'=32] {'aux'}, dimensions={1} | all-to-all | bytes 1048576 | tf_op jit(solution)/shard_map/all_to_all | solution.py:44
  245.9 12.6 %all-to-all-start.3 = ((f32[16,32,512]{2,1,0:T(8,128)}), f32[16,32,512]{2,1,0:T(8,128)}, u32[]{:S(2)}, u32[]{:S(2)}) async-start(f32[16,32,512]{2,1,0:T(8,128)} %stack.5), calls=%async_computation.3 | async-start | bytes 2097152 | tf_op jit(solution)/shard_map/all_to_all | solution.py:12
  258.6 3.2 fusion.21
  261.8 42.1 %all-to-all-done.3 = f32[16,32,512]{2,1,0:T(8,128)} async-done(((f32[16,32,512]{2,1,0:T(8,128)}), f32[16,32,512]{2,1,0:T(8,128)}, u32[]{:S(2)}, u32[]{:S(2)}) %all-to-all-start.3) | async-done | bytes 1048608 | tf_op jit(solution)/shard_map/all_to_all | solution.py:12
  303.9 1.4 copy.31
  307.4 29.6 %all-gather.3 = f32[1024,32]{1,0:T(8,128)S(1)} all-gather(f32[32,32]{1,0:T(8,128)S(1)} %copy.21), channel_id=5, replica_groups=mesh['aux'=16,'pair'=32] {'pair'}, dimensions={0}, use_global_device_ids=true | all-gather | bytes 135168 | tf_op jit(solution)/shard_map/all_gather | solution.py:37
  337.0 4.3 %fusion.18 = (bf16[32,8192]{1,0:T(8,128)(2,1)}, f32[32,8192]{1,0:T(8,128)}) fusion(f32[32,8192]{1,0:T(8,128)} %fusion.21, f32[8192]{0:T(1024)S(1)} %dynamic_slice.3, f32[32,32]{1,0:T(8,128)S(1)} %reduce_sum.59, f32[32,8192]{1,0:T(8,128)} %bitcast.68), kind=kOutput, calls=%fused_computation.48 | convolution fusion | flops 102236160 | bytes 3706880 | tf_op jit(solution)/shard_map/dot_general | solution.py:31
  (57 shorter events, 17.1 us)
Async XLA Ops:
  0.6 2.1 copy-start
  45.6 49.1 %copy-start.8 = (f32[1024]{0:T(1024)S(1)}, f32[1024]{0:T(1024)}, u32[]{:S(2)}) copy-start(f32[1024]{0:T(1024)} %param.9) | copy-start | bytes 12292
  45.6 49.1 %copy-start.9 = (f32[256]{0:T(256)S(1)}, f32[256]{0:T(256)}, u32[]{:S(2)}) copy-start(f32[256]{0:T(256)} %param.8) | copy-start | bytes 3076
  82.0 14.9 %copy-start.4 = (bf16[32,8192]{1,0:T(8,128)(2,1)S(1)}, bf16[32,8192]{1,0:T(8,128)(2,1)}, u32[]{:S(2)}) copy-start(bf16[32,8192]{1,0:T(8,128)(2,1)} %param.10) | copy-start | bytes 1572868
  82.0 58.1 %all-to-all-start.1 = ((f32[16,32,512]{2,1,0:T(8,128)}), f32[16,32,512]{2,1,0:T(8,128)}, u32[]{:S(2)}, u32[]{:S(2)}) async-start(f32[16,32,512]{2,1,0:T(8,128)} %stack.4), calls=%async_computation.1 | async-start | bytes 2097152 | tf_op jit(solution)/shard_map/all_to_all | solution.py:12
  140.0 2.4 copy-start.3
  141.4 1.0 copy-start.6
  176.2 3.4 %copy-start.1 = (f32[32,8192]{1,0:T(8,128)}, f32[32,8192]{1,0:T(8,128)S(1)}, u32[]{:S(2)}) copy-start(f32[32,8192]{1,0:T(8,128)S(1)} %fusion.1) | copy-start | bytes 3145732
  245.9 57.9 %all-to-all-start.3 = ((f32[16,32,512]{2,1,0:T(8,128)}), f32[16,32,512]{2,1,0:T(8,128)}, u32[]{:S(2)}, u32[]{:S(2)}) async-start(f32[16,32,512]{2,1,0:T(8,128)} %stack.5), calls=%async_computation.3 | async-start | bytes 2097152 | tf_op jit(solution)/shard_map/all_to_all | solution.py:12
  303.9 2.4 copy-start.2
  305.3 1.0 copy-start.5
  337.0 4.3 %copy-start.7 = (f32[32,32]{1,0:T(8,128)}, f32[32,32]{1,0:T(8,128)S(1)}, u32[]{:S(2)}) copy-start(f32[32,32]{1,0:T(8,128)S(1)} %reduce_sum.59) | copy-start | bytes 12292
